TPU v7x, 32 devices: a whole 2x2x4 slice. The times are simulated.
32 devices in a mesh: blk: 8 (over z, y), uly: 4 (over x, core).
Axes of the slice: x: 2, y: 2, z: 4, core: 2. Of those that a mesh axis runs over, the one named last changes fastest.
Arguments:
- tokens: bfloat16 [8, 16, 8, 1024], P('blk', None, 'uly'), may hold values from -12 to 12, as said below
- conv_weight: float32 [27, 1024], replicated, may hold values from -1.2 to 1.2
- conv_bias: float32 [1024], replicated, may hold values from -3 to 3
- qkv_weight: bfloat16 [3072, 1024], P('uly'), may hold values from -0.25 to 0.25
- out_weight: bfloat16 [1024, 1024], P('uly'), may hold values from -1.5 to 1.5
Outputs:
- attended_out: bfloat16 [8, 16, 8, 1024], P('blk', None, 'uly')
Inputs may be any that keep to these rules, and one draw needn't show every extreme that they name: `tokens`: patch embeddings of the subvolume.
All inputs are finite; a program needn't handle non-finite values.
Results may differ from a plain program's by a relative error of at most 0.012.
The roundings to bfloat16 on the way count: a program that leaves them out, or rounds other values in their place, can miss the bound.
Values may be sent and summed in bfloat16 or wider, within the bound.
No kernel may reach another device: no remote copies, remote signals or barrier semaphores. Data moves between devices by JAX's collectives and lax.ppermute only.
A program may use at most 64 MiB of HBM per device.

v0:
```python
import math
import jax
import jax.numpy as jnp
from jax import lax
from jax.sharding import PartitionSpec as P

HS = 64


def padded_2(shard, sides, width):
    for axis, dim in sides:
        size, length = (lax.axis_size(axis), shard.shape[dim])
        up = [(i, (i + 1) % size) for i in range(size - 1)]
        down = [(j, i) for i, j in up]
        last = lax.slice_in_dim(shard, length - width, length, axis=dim)
        initial = lax.slice_in_dim(shard, 0, width, axis=dim)
        before = lax.ppermute(last, axis, up)
        after = lax.ppermute(initial, axis, down)
        shard = jnp.concatenate([before, shard, after], axis=dim)
    return shard


def times_transposed(left, right):
    return lax.dot_general(
        left, right, (((1,), (1,)), ((), ())), preferred_element_type=jnp.float32
    )


def on_device(tokens, conv_weight, conv_bias, qkv_weight, out_weight):
    z_count, x_count, y_count, features = tokens.shape
    padded = padded_2(tokens, (("blk", 0), ("uly", 2)), 1)
    padded = jnp.pad(padded, ((0, 0), (1, 1), (0, 0), (0, 0)))
    summed = tokens.astype(jnp.float32) + conv_bias
    for step_z in range(3):
        for step_x in range(3):
            for step_y in range(3):
                summed = (
                    summed
                    + conv_weight[9 * step_z + 3 * step_x + step_y]
                    * padded[
                        step_z : step_z + z_count,
                        step_x : step_x + x_count,
                        step_y : step_y + y_count,
                    ]
                )
    token_rows = summed.astype(jnp.bfloat16).reshape(-1, features)
    local_tok = token_rows.shape[0]
    heads_here = qkv_weight.shape[0] // (3 * HS)
    slab_rows = lax.all_gather(token_rows, "uly", axis=0, tiled=True)
    slab_tok = slab_rows.shape[0]
    projected = times_transposed(slab_rows, qkv_weight).astype(jnp.bfloat16)
    split_heads = projected.reshape(slab_tok, heads_here, 3, HS)
    queries = split_heads[:, :, 0]
    key_rows = split_heads[:, :, 1]
    val_rows = split_heads[:, :, 2]
    score_scale = 1.0 / math.sqrt(HS)

    def key_block(carry_state, key_value):
        running_max, running_sum, weighted = carry_state
        key_part, value_part = key_value
        scores = (
            jnp.einsum("qhd,khd->hqk", queries, key_part, preferred_element_type=jnp.float32)
            * score_scale
        )
        new_max = jnp.maximum(running_max, jnp.max(scores, axis=2))
        shrink = jnp.exp(running_max - new_max)
        weights = jnp.exp(scores - new_max[:, :, None])
        running_sum = running_sum * shrink + jnp.sum(weights, axis=2)
        weighted = weighted * shrink[:, :, None] + jnp.einsum(
            "hqk,khd->hqd",
            weights.astype(jnp.bfloat16),
            value_part,
            preferred_element_type=jnp.float32,
        )
        return ((new_max, running_sum, weighted), None)

    start_state = (
        jnp.full((heads_here, slab_tok), -1e30, jnp.float32),
        jnp.zeros((heads_here, slab_tok), jnp.float32),
        jnp.zeros((heads_here, slab_tok, HS), jnp.float32),
    )
    key_piece = lax.all_gather(key_rows, "blk", axis=0, tiled=True)
    value_piece = lax.all_gather(val_rows, "blk", axis=0, tiled=True)
    key_count = key_piece.shape[0]
    block_len = min(1024, key_count)
    key_blocks = key_piece.reshape(key_count // block_len, block_len, heads_here, HS)
    value_blocks = value_piece.reshape(key_count // block_len, block_len, heads_here, HS)
    folded, unused = lax.scan(key_block, start_state, (key_blocks, value_blocks))
    running_max, running_sum, weighted = folded
    attended = (weighted / running_sum[:, :, None]).astype(jnp.bfloat16)
    head_rows = attended.transpose(1, 0, 2).reshape(slab_tok, heads_here * HS)
    partial = jnp.dot(head_rows, out_weight, preferred_element_type=jnp.float32)
    result = lax.psum_scatter(partial, "uly", scatter_dimension=0, tiled=True)
    return result.astype(jnp.bfloat16).reshape(z_count, x_count, y_count, features)


def solution(mesh):
    in_specs = (P("blk", None, "uly", None), P(), P(), P("uly", None), P("uly", None))
    out_specs = P("blk", None, "uly", None)
    return jax.shard_map(
        on_device, mesh=mesh, in_specs=in_specs, out_specs=out_specs, check_vma=False
    )
```

profile of v0, /device:TPU:0, one launch (start us, length us, event | category | flops | bytes accessed | tf_op | source)
XLA Modules:
  0.0 123.3 jit_solution(7568137373259578012)
XLA Ops:
  6.5 0.0 copy-start
  6.5 0.0 reduce-scatter.2.cloned.1.call-start
  6.5 5.0 %collective-permute-start = (bf16[1,16,2,1024]{3,2,1,0:T(2,128)(2,1)}, bf16[1,16,2,1024]{3,2,1,0:T(2,128)(2,1)S(1)}, u32[]{:S(2)}, u32[]{:S(2)}) collective-permute-start(bf16[1,16,2,1024]{3,2,1,0:T(2,128)(2,1)} %param.5), channel_id=1, source_target_pairs={{0,4},{4,8},{8,12},{12,16},{16,20},{20,24},{24,28},{1,5},{5,9},{9,... | collective-permute-start | bytes 196616 | tf_op jit(solution)/shard_map/ppermute | solution.py:17
  11.6 1.3 %collective-permute-start.1 = (bf16[1,16,2,1024]{3,2,1,0:T(2,128)(2,1)}, bf16[1,16,2,1024]{3,2,1,0:T(2,128)(2,1)S(1)}, u32[]{:S(2)}, u32[]{:S(2)}) collective-permute-start(bf16[1,16,2,1024]{3,2,1,0:T(2,128)(2,1)} %param.5), channel_id=1, source_target_pairs={{4,0},{8,4},{12,8},{16,12},{20,16},{24,20},{28,24},{5,1},{9,5},{13... | collective-permute-start | bytes 196616 | tf_op jit(solution)/shard_map/ppermute | solution.py:18
  12.9 1.4 %fusion.26 = (f32[1,1024]{1,0:T(1,128)S(1)}, f32[1,1024]{1,0:T(1,128)S(1)}, f32[1,1024]{1,0:T(1,128)S(1)}, f32[1,1024]{1,0:T(1,128)S(1)}, f32[1,1024]{1,0:T(1,12...) fusion(f32[27,1024]{1,0:T(8,128)} %param.6), kind=kLoop, calls=%fused_computation.47 | loop fusion | bytes 155648 | tf_op jit(solution)/shard_map/slice | solution.py:39
  14.3 0.0 collective-permute-done
  14.3 0.9 constant_dynamic-update-slice_fusion.1
  15.2 2.7 %collective-permute-done.1 = bf16[1,16,2,1024]{3,2,1,0:T(2,128)(2,1)S(1)} collective-permute-done((bf16[1,16,2,1024]{3,2,1,0:T(2,128)(2,1)}, bf16[1,16,2,1024]{3,2,1,0:T(2,128)(2,1)S(1)}, u32[]{:S(2)}, u32[]{:S(2)}) %collective-permute-start.1) | collective-permute-done | bytes 65568 | tf_op jit(solution)/shard_map/ppermute | solution.py:18
  17.9 0.1 constant_dynamic-update-slice_fusion
  18.0 0.3 fusion.25
  18.3 1.3 %collective-permute-start.2 = (bf16[3,16,1,1024]{3,2,1,0:T(2,128)(2,1)S(1)}, bf16[3,16,1,1024]{3,2,1,0:T(2,128)(2,1)S(1)}, u32[]{:S(2)}, u32[]{:S(2)}) collective-permute-start(bf16[3,16,1,1024]{3,2,1,0:T(2,128)(2,1)S(1)} %get-tuple-element.19), channel_id=1, source_target_pairs={{0,1},{1,2},{2,3},{4,5},{5,6},{6,7},{8,9},{9,10},{10,11},{12,13},{... | collective-permute-start | bytes 294920 | tf_op jit(solution)/shard_map/ppermute | solution.py:17
  19.6 1.3 %collective-permute-start.3 = (bf16[3,16,1,1024]{3,2,1,0:T(2,128)(2,1)S(1)}, bf16[3,16,1,1024]{3,2,1,0:T(2,128)(2,1)S(1)}, u32[]{:S(2)}, u32[]{:S(2)}) collective-permute-start(bf16[3,16,1,1024]{3,2,1,0:T(2,128)(2,1)S(1)} %get-tuple-element.20), channel_id=1, source_target_pairs={{1,0},{2,1},{3,2},{5,4},{6,5},{7,6},{9,8},{10,9},{11,10},{13,12},{... | collective-permute-start | bytes 294920 | tf_op jit(solution)/shard_map/ppermute | solution.py:18
  20.9 1.2 fusion.27
  22.1 0.0 collective-permute-done.2
  22.1 2.6 %collective-permute-done.3 = bf16[3,16,1,1024]{3,2,1,0:T(2,128)(2,1)S(1)} collective-permute-done((bf16[3,16,1,1024]{3,2,1,0:T(2,128)(2,1)S(1)}, bf16[3,16,1,1024]{3,2,1,0:T(2,128)(2,1)S(1)}, u32[]{:S(2)}, u32[]{:S(2)}) %collective-permute-start.3) | collective-permute-done | bytes 98336 | tf_op jit(solution)/shard_map/ppermute | solution.py:18
  24.6 0.7 select_maximum_fusion
  25.3 0.0 copy-done.2
  25.3 0.0 copy-done.3
  25.3 2.5 %add_convert_fusion = bf16[1,16,2,1024]{3,2,1,0:T(2,128)(2,1)S(1)} fusion(bf16[1,16,2,1024]{3,2,1,0:T(2,128)(2,1)S(1)} %collective-permute-done.1, bf16[1,16,2,1024]{3,2,1,0:T(2,128)(2,1)S(1)} %copy-done.2, bf16[1,16,2,1024]{3,2,1,0:T(2,128)(2,1)S(1)} %collective-permute-done, bf16[3,18,4,1024]{3,2,1,0:T(4,128)(2,1)S(1)} %select_maximum_fusion, ...), kind=kLoop, calls=%fused_computation.33 | loop fusion | flops 3309568 | bytes 1949696 | tf_op jit(solution)/shard_map/convert_element_type | solution.py:46
  27.8 8.6 %all_gather.9 = bf16[128,1024]{1,0:T(8,128)(2,1)S(1)} all-gather(bf16[32,1024]{1,0:T(8,128)(2,1)S(1)} %reshape.115), channel_id=1, replica_groups=mesh['blk'=8,'uly'=4] {'uly'}, dimensions={0}, use_global_device_ids=true | all-gather | bytes 327680 | tf_op jit(solution)/shard_map/all_gather | solution.py:49
  36.5 0.7 convolution_convert_fusion
  37.1 0.2 copy.9
  37.3 28.0 %all-gather = bf16[1024,4,1,64]{0,3,1,2:T(8,128)(2,1)S(1)} all-gather(bf16[128,4,1,64]{0,3,1,2:T(8,128)(2,1)S(1)} %get-tuple-element.18), channel_id=2, replica_groups=mesh['blk'=8,'uly'=4] {'blk'}, dimensions={0}, use_global_device_ids=true | all-gather | bytes 589824 | tf_op jit(solution)/shard_map/all_gather | solution.py:82
  65.3 0.6 multiply_reduce_fusion
  65.9 0.5 fusion
  66.5 27.7 %all-gather.1 = bf16[1024,4,1,64]{0,3,1,2:T(8,128)(2,1)S(1)} all-gather(bf16[128,4,1,64]{0,3,1,2:T(8,128)(2,1)S(1)} %get-tuple-element.17), channel_id=3, replica_groups=mesh['blk'=8,'uly'=4] {'blk'}, dimensions={0}, use_global_device_ids=true | all-gather | bytes 589824 | tf_op jit(solution)/shard_map/all_gather | solution.py:83
  94.2 0.6 fusion.4
  94.8 1.1 fusion.28
  95.9 0.0 reduce-scatter.2.cloned.1.call-update
  95.9 19.0 %reduce-scatter.2.cloned.1.call-done = f32[32,1024]{1,0:T(8,128)} async-done(((f32[128,1024]{1,0:T(8,128)}), f32[32,1024]{1,0:T(8,128)}) %reduce-scatter.2.cloned.1.call-update) | async-done | bytes 131088 | tf_op jit(solution)/shard_map/reduce_scatter | solution.py:93
  114.9 0.9 convert_element_type.132
  115.8 0.7 reshape.118
  (10 shorter events, 0.1 us)
Async XLA Ops:
  6.5 29.9 %copy-start = (bf16[768,1024]{1,0:T(8,128)(2,1)S(1)}, bf16[768,1024]{1,0:T(8,128)(2,1)}, u32[]{:S(2)}) copy-start(bf16[768,1024]{1,0:T(8,128)(2,1)} %param.8) | copy-start | bytes 4718596
  6.5 18.8 %copy-start.2 = (bf16[1,16,2,1024]{3,2,1,0:T(2,128)(2,1)S(1)}, bf16[1,16,2,1024]{3,2,1,0:T(2,128)(2,1)}, u32[]{:S(2)}) copy-start(bf16[1,16,2,1024]{3,2,1,0:T(2,128)(2,1)} %param.5) | copy-start | bytes 196612
  6.5 18.8 %copy-start.3 = (f32[1024]{0:T(1024)S(1)}, f32[1024]{0:T(1024)}, u32[]{:S(2)}) copy-start(f32[1024]{0:T(1024)} %param.7) | copy-start | bytes 12292
  6.5 108.4 %reduce-scatter.2.cloned.1.call-start = ((), (), s32[]{:S(2)}) async-start(), calls=%async_computation.1 | async-start | bytes 655360 | tf_op jit(solution)/shard_map/reduce_scatter | solution.py:93
  6.5 7.7 %collective-permute-start = (bf16[1,16,2,1024]{3,2,1,0:T(2,128)(2,1)}, bf16[1,16,2,1024]{3,2,1,0:T(2,128)(2,1)S(1)}, u32[]{:S(2)}, u32[]{:S(2)}) collective-permute-start(bf16[1,16,2,1024]{3,2,1,0:T(2,128)(2,1)} %param.5), channel_id=1, source_target_pairs={{0,4},{4,8},{8,12},{12,16},{16,20},{20,24},{24,28},{1,5},{5,9},{9,... | collective-permute-start | bytes 196616 | tf_op jit(solution)/shard_map/ppermute | solution.py:17
  11.6 6.4 %collective-permute-start.1 = (bf16[1,16,2,1024]{3,2,1,0:T(2,128)(2,1)}, bf16[1,16,2,1024]{3,2,1,0:T(2,128)(2,1)S(1)}, u32[]{:S(2)}, u32[]{:S(2)}) collective-permute-start(bf16[1,16,2,1024]{3,2,1,0:T(2,128)(2,1)} %param.5), channel_id=1, source_target_pairs={{4,0},{8,4},{12,8},{16,12},{20,16},{24,20},{28,24},{5,1},{9,5},{13... | collective-permute-start | bytes 196616 | tf_op jit(solution)/shard_map/ppermute | solution.py:18
  18.3 3.8 %collective-permute-start.2 = (bf16[3,16,1,1024]{3,2,1,0:T(2,128)(2,1)S(1)}, bf16[3,16,1,1024]{3,2,1,0:T(2,128)(2,1)S(1)}, u32[]{:S(2)}, u32[]{:S(2)}) collective-permute-start(bf16[3,16,1,1024]{3,2,1,0:T(2,128)(2,1)S(1)} %get-tuple-element.19), channel_id=1, source_target_pairs={{0,1},{1,2},{2,3},{4,5},{5,6},{6,7},{8,9},{9,10},{10,11},{12,13},{... | collective-permute-start | bytes 294920 | tf_op jit(solution)/shard_map/ppermute | solution.py:17
  19.6 5.1 %collective-permute-start.3 = (bf16[3,16,1,1024]{3,2,1,0:T(2,128)(2,1)S(1)}, bf16[3,16,1,1024]{3,2,1,0:T(2,128)(2,1)S(1)}, u32[]{:S(2)}, u32[]{:S(2)}) collective-permute-start(bf16[3,16,1,1024]{3,2,1,0:T(2,128)(2,1)S(1)} %get-tuple-element.20), channel_id=1, source_target_pairs={{1,0},{2,1},{3,2},{5,4},{6,5},{7,6},{9,8},{10,9},{11,10},{13,12},{... | collective-permute-start | bytes 294920 | tf_op jit(solution)/shard_map/ppermute | solution.py:18
  66.4 28.4 %copy-start.1 = (bf16[256,1024]{1,0:T(8,128)(2,1)S(1)}, bf16[256,1024]{1,0:T(8,128)(2,1)}, u32[]{:S(2)}) copy-start(bf16[256,1024]{1,0:T(8,128)(2,1)} %param.9) | copy-start | bytes 1572868
Sparse Core Ops, SparseCore 0:
  96.0 18.8 reduce-scatter.1
where the time goes:
time: 124 us; the launch traced here: 123 us
  blocking collectives  64.4 us (52%)
  waiting for transfers between devices  24.3 us (20%)
  between operations  13.5 us (11%)
  starting transfers between devices  8.9 us (7%)
  local copies, waits for them, and re-layouts  4.73 us (4%)
  other arithmetic  4.58 us (4%)
  matrix products  2.88 us (2%)
    all_gather x1, blocking collectives, on_device(): key_piece = lax.all_gather(key_rows, 'blk', axis=0, tiled=True)  28 us
    all_gather x1, blocking collectives, on_device(): value_piece = lax.all_gather(val_rows, 'blk', axis=0, tiled=True)  27.7 us
    reduce_scatter x1, waiting for transfers between devices, on_device(): result = lax.psum_scatter(partial, 'uly', scatter_dimension=0, tiled=True)  19 us
    all_gather x1, blocking collectives, on_device(): slab_rows = lax.all_gather(token_rows, 'uly', axis=0, tiled=True)  8.62 us
    ppermute x2, starting transfers between devices, padded_2(): before = lax.ppermute(last, axis, up)  6.31 us
    ppermute x2, waiting for transfers between devices, padded_2(): after = lax.ppermute(initial, axis, down)  5.26 us
    ppermute x2, starting transfers between devices, padded_2(): after = lax.ppermute(initial, axis, down)  2.58 us
    slice x2, local copies, waits for them, and re-layouts, on_device(): conv_weight[9 * step_z + 3 * step_x + step_y]  2.58 us
  transfers between devices with their start and end apart: 5, of which 3 were waited for; matrix products, arithmetic and copies ran while one was open for 3% of the time, Pallas kernels for 0%

commit v1 on v0

--- a/solution.py
+++ b/solution.py
@@ -79,8 +79,11 @@
         jnp.zeros((heads_here, slab_tok), jnp.float32),
         jnp.zeros((heads_here, slab_tok, HS), jnp.float32),
     )
-    key_piece = lax.all_gather(key_rows, "blk", axis=0, tiled=True)
-    value_piece = lax.all_gather(val_rows, "blk", axis=0, tiled=True)
+    key_piece, value_piece = jnp.split(
+        lax.all_gather(jnp.concatenate([key_rows, val_rows], axis=1), "blk", axis=0, tiled=True),
+        [key_rows.shape[1]],
+        axis=1,
+    )
     key_count = key_piece.shape[0]
     block_len = min(1024, key_count)
     key_blocks = key_piece.reshape(key_count // block_len, block_len, heads_here, HS)

time: 124 us -> 113 us (0.911)
  blocking collectives: 64.4 us -> 8.62 us
  waiting for transfers between devices: 24.3 us -> 66.6 us
    all_gather x2 -> x0, blocking collectives: 55.7 us -> none  [the longest x1 28 us: on_device(): key_piece = lax.all_gather(key_rows, 'blk', axis=0, tiled=True)]
    all_gather x0 -> x1, waiting for transfers between devices: none -> 40.6 us  [on_device(): lax.all_gather(jnp.concatenate([key_rows, val_rows], axis=1), 'blk', axis...]
    reduce_scatter x1, waiting for transfers between devices: 19 us -> 20.7 us  [on_device(): result = lax.psum_scatter(partial, 'uly', scatter_dimension=0, tiled=True)]
  transfers between devices with their start and end apart: 5 -> 6, of which waited for: 3 -> 4; matrix products, arithmetic and copies ran while one was open for 3% -> 3% of each run, Pallas kernels for 0% -> 0%
where the time goes in v1:
time: 113 us; the launch traced here: 112 us
  waiting for transfers between devices  66.6 us (59%)
  between operations  13.6 us (12%)
  starting transfers between devices  8.94 us (8%)
  blocking collectives  8.62 us (8%)
  other arithmetic  5.24 us (5%)
  local copies, waits for them, and re-layouts  5.14 us (5%)
  matrix products  4 us (4%)
    all_gather x1, waiting for transfers between devices, on_device(): lax.all_gather(jnp.concatenate([key_rows, val_rows], axis=1), 'blk', axis...  40.6 us
    reduce_scatter x1, waiting for transfers between devices, on_device(): result = lax.psum_scatter(partial, 'uly', scatter_dimension=0, tiled=True)  20.7 us
    all_gather x1, blocking collectives, on_device(): slab_rows = lax.all_gather(token_rows, 'uly', axis=0, tiled=True)  8.62 us
    ppermute x2, starting transfers between devices, padded_2(): before = lax.ppermute(last, axis, up)  6.31 us
    ppermute x2, waiting for transfers between devices, padded_2(): after = lax.ppermute(initial, axis, down)  5.26 us
    ppermute x2, starting transfers between devices, padded_2(): after = lax.ppermute(initial, axis, down)  2.58 us
    slice x2, local copies, waits for them, and re-layouts, on_device(): conv_weight[9 * step_z + 3 * step_x + step_y]  2.58 us
    convert_element_type x1, other arithmetic, on_device(): token_rows = summed.astype(jnp.bfloat16).reshape(-1, features)  2.46 us
  transfers between devices with their start and end apart: 6, of which 4 were waited for; matrix products, arithmetic and copies ran while one was open for 3% of the time, Pallas kernels for 0%

profile of v1, /device:TPU:0, one launch (start us, length us, event | category | flops | bytes accessed | tf_op | source)
XLA Modules:
  0.0 112.1 jit_solution(15321847649376989015)
XLA Ops:
  6.5 0.0 copy-start
  6.5 5.0 %collective-permute-start = (bf16[1,16,2,1024]{3,2,1,0:T(2,128)(2,1)}, bf16[1,16,2,1024]{3,2,1,0:T(2,128)(2,1)S(1)}, u32[]{:S(2)}, u32[]{:S(2)}) collective-permute-start(bf16[1,16,2,1024]{3,2,1,0:T(2,128)(2,1)} %param.5), channel_id=1, source_target_pairs={{0,4},{4,8},{8,12},{12,16},{16,20},{20,24},{24,28},{1,5},{5,9},{9,... | collective-permute-start | bytes 196616 | tf_op jit(solution)/shard_map/ppermute | solution.py:17
  11.6 1.3 %collective-permute-start.1 = (bf16[1,16,2,1024]{3,2,1,0:T(2,128)(2,1)}, bf16[1,16,2,1024]{3,2,1,0:T(2,128)(2,1)S(1)}, u32[]{:S(2)}, u32[]{:S(2)}) collective-permute-start(bf16[1,16,2,1024]{3,2,1,0:T(2,128)(2,1)} %param.5), channel_id=1, source_target_pairs={{4,0},{8,4},{12,8},{16,12},{20,16},{24,20},{28,24},{5,1},{9,5},{13... | collective-permute-start | bytes 196616 | tf_op jit(solution)/shard_map/ppermute | solution.py:18
  12.9 1.4 %fusion.26 = (f32[1,1024]{1,0:T(1,128)S(1)}, f32[1,1024]{1,0:T(1,128)S(1)}, f32[1,1024]{1,0:T(1,128)S(1)}, f32[1,1024]{1,0:T(1,128)S(1)}, f32[1,1024]{1,0:T(1,12...) fusion(f32[27,1024]{1,0:T(8,128)} %param.6), kind=kLoop, calls=%fused_computation.48 | loop fusion | bytes 155648 | tf_op jit(solution)/shard_map/slice | solution.py:39
  14.3 0.0 collective-permute-done
  14.3 0.9 constant_dynamic-update-slice_fusion.1
  15.2 2.7 %collective-permute-done.1 = bf16[1,16,2,1024]{3,2,1,0:T(2,128)(2,1)S(1)} collective-permute-done((bf16[1,16,2,1024]{3,2,1,0:T(2,128)(2,1)}, bf16[1,16,2,1024]{3,2,1,0:T(2,128)(2,1)S(1)}, u32[]{:S(2)}, u32[]{:S(2)}) %collective-permute-start.1) | collective-permute-done | bytes 65568 | tf_op jit(solution)/shard_map/ppermute | solution.py:18
  17.9 0.1 constant_dynamic-update-slice_fusion
  18.0 0.3 fusion.25
  18.3 1.3 %collective-permute-start.2 = (bf16[3,16,1,1024]{3,2,1,0:T(2,128)(2,1)S(1)}, bf16[3,16,1,1024]{3,2,1,0:T(2,128)(2,1)S(1)}, u32[]{:S(2)}, u32[]{:S(2)}) collective-permute-start(bf16[3,16,1,1024]{3,2,1,0:T(2,128)(2,1)S(1)} %get-tuple-element.19), channel_id=1, source_target_pairs={{0,1},{1,2},{2,3},{4,5},{5,6},{6,7},{8,9},{9,10},{10,11},{12,13},{... | collective-permute-start | bytes 294920 | tf_op jit(solution)/shard_map/ppermute | solution.py:17
  19.6 1.3 %collective-permute-start.3 = (bf16[3,16,1,1024]{3,2,1,0:T(2,128)(2,1)S(1)}, bf16[3,16,1,1024]{3,2,1,0:T(2,128)(2,1)S(1)}, u32[]{:S(2)}, u32[]{:S(2)}) collective-permute-start(bf16[3,16,1,1024]{3,2,1,0:T(2,128)(2,1)S(1)} %get-tuple-element.20), channel_id=1, source_target_pairs={{1,0},{2,1},{3,2},{5,4},{6,5},{7,6},{9,8},{10,9},{11,10},{13,12},{... | collective-permute-start | bytes 294920 | tf_op jit(solution)/shard_map/ppermute | solution.py:18
  20.9 1.2 %fusion.27 = (f32[1,1024]{1,0:T(1,128)S(1)}, f32[1,1024]{1,0:T(1,128)S(1)}, f32[1,1024]{1,0:T(1,128)S(1)}, f32[1,1024]{1,0:T(1,128)S(1)}, f32[1,1024]{1,0:T(1,12...) fusion(f32[27,1024]{1,0:T(8,128)} %param.6), kind=kLoop, calls=%fused_computation.49 | loop fusion | bytes 65536 | tf_op jit(solution)/shard_map/slice | solution.py:39
  22.1 0.0 collective-permute-done.2
  22.1 2.6 %collective-permute-done.3 = bf16[3,16,1,1024]{3,2,1,0:T(2,128)(2,1)S(1)} collective-permute-done((bf16[3,16,1,1024]{3,2,1,0:T(2,128)(2,1)S(1)}, bf16[3,16,1,1024]{3,2,1,0:T(2,128)(2,1)S(1)}, u32[]{:S(2)}, u32[]{:S(2)}) %collective-permute-start.3) | collective-permute-done | bytes 98336 | tf_op jit(solution)/shard_map/ppermute | solution.py:18
  24.6 0.7 select_maximum_fusion
  25.3 2.5 %add_convert_fusion = bf16[1,16,2,1024]{3,2,1,0:T(2,128)(2,1)S(1)} fusion(bf16[1,16,2,1024]{3,2,1,0:T(2,128)(2,1)S(1)} %collective-permute-done.1, bf16[1,16,2,1024]{3,2,1,0:T(2,128)(2,1)S(1)} %copy-done.2, bf16[1,16,2,1024]{3,2,1,0:T(2,128)(2,1)S(1)} %collective-permute-done, bf16[3,18,4,1024]{3,2,1,0:T(4,128)(2,1)S(1)} %select_maximum_fusion, ...), kind=kLoop, calls=%fused_computation.34 | loop fusion | flops 3309568 | bytes 1949696 | tf_op jit(solution)/shard_map/convert_element_type | solution.py:46
  27.8 8.6 %all_gather.6 = bf16[128,1024]{1,0:T(8,128)(2,1)S(1)} all-gather(bf16[32,1024]{1,0:T(8,128)(2,1)S(1)} %reshape.115), channel_id=1, replica_groups=mesh['blk'=8,'uly'=4] {'uly'}, dimensions={0}, use_global_device_ids=true | all-gather | bytes 327680 | tf_op jit(solution)/shard_map/all_gather | solution.py:49
  36.5 0.7 convolution_convert_fusion
  37.1 0.2 copy.9
  37.3 0.7 pad_maximum_fusion
  38.0 0.0 all-gather.2.cloned.1.call-update
  38.0 0.0 reduce-scatter.2.cloned.1.call-start
  38.0 40.6 %all-gather.2.cloned.1.call-done = bf16[1024,8,64]{0,2,1:T(8,128)(2,1)} async-done(((bf16[128,8,64]{0,2,1:T(8,128)(2,1)}), bf16[1024,8,64]{0,2,1:T(8,128)(2,1)}) %all-gather.2.cloned.1.call-update) | async-done | bytes 1048592 | tf_op jit(solution)/shard_map/all_gather | solution.py:83
  78.7 1.7 %multiply_reduce_fusion = (f32[4,128]{1,0:T(4,128)S(1)}, f32[4,128,1024]{2,1,0:T(8,128)S(1)}) fusion(bf16[1024,8,64]{0,2,1:T(8,128)(2,1)} %all-gather.2.cloned.1.call-done, bf16[128,4,3,64]{0,3,2,1:T(8,128)(2,1)S(1)} %bitcast.63), kind=kOutput, calls=%fused_computation.1 | convolution fusion | flops 68156928 | bytes 2689024 | tf_op jit(solution)/shard_map/while/body/eval_jaxpr/qhd,khd->hqk/dot_general | solution.py:62
  80.4 0.5 fusion
  80.9 0.6 fusion.4
  81.5 0.4 copy-done.1
  81.9 1.1 fusion.28
  83.0 0.0 reduce-scatter.2.cloned.1.call-update
  83.0 20.7 %reduce-scatter.2.cloned.1.call-done = f32[32,1024]{1,0:T(8,128)} async-done(((f32[128,1024]{1,0:T(8,128)}), f32[32,1024]{1,0:T(8,128)}) %reduce-scatter.2.cloned.1.call-update) | async-done | bytes 131088 | tf_op jit(solution)/shard_map/reduce_scatter | solution.py:96
  103.7 0.9 convert_element_type.132
  104.6 0.7 reshape.118
  (14 shorter events, 0.1 us)
Async XLA Ops:
  6.5 29.9 %copy-start = (bf16[768,1024]{1,0:T(8,128)(2,1)S(1)}, bf16[768,1024]{1,0:T(8,128)(2,1)}, u32[]{:S(2)}) copy-start(bf16[768,1024]{1,0:T(8,128)(2,1)} %param.8) | copy-start | bytes 4718596
  6.5 18.8 %copy-start.2 = (bf16[1,16,2,1024]{3,2,1,0:T(2,128)(2,1)S(1)}, bf16[1,16,2,1024]{3,2,1,0:T(2,128)(2,1)}, u32[]{:S(2)}) copy-start(bf16[1,16,2,1024]{3,2,1,0:T(2,128)(2,1)} %param.5) | copy-start | bytes 196612
  6.5 18.8 %copy-start.4 = (f32[1024]{0:T(1024)S(1)}, f32[1024]{0:T(1024)}, u32[]{:S(2)}) copy-start(f32[1024]{0:T(1024)} %param.7) | copy-start | bytes 12292
  6.5 72.1 %all-gather.2.cloned.1.call-start = ((), (), s32[]{:S(2)}) async-start(), calls=%async_computation.1 | async-start | bytes 1179648 | tf_op jit(solution)/shard_map/all_gather | solution.py:83
  6.5 7.7 %collective-permute-start = (bf16[1,16,2,1024]{3,2,1,0:T(2,128)(2,1)}, bf16[1,16,2,1024]{3,2,1,0:T(2,128)(2,1)S(1)}, u32[]{:S(2)}, u32[]{:S(2)}) collective-permute-start(bf16[1,16,2,1024]{3,2,1,0:T(2,128)(2,1)} %param.5), channel_id=1, source_target_pairs={{0,4},{4,8},{8,12},{12,16},{16,20},{20,24},{24,28},{1,5},{5,9},{9,... | collective-permute-start | bytes 196616 | tf_op jit(solution)/shard_map/ppermute | solution.py:17
  11.6 6.4 %collective-permute-start.1 = (bf16[1,16,2,1024]{3,2,1,0:T(2,128)(2,1)}, bf16[1,16,2,1024]{3,2,1,0:T(2,128)(2,1)S(1)}, u32[]{:S(2)}, u32[]{:S(2)}) collective-permute-start(bf16[1,16,2,1024]{3,2,1,0:T(2,128)(2,1)} %param.5), channel_id=1, source_target_pairs={{4,0},{8,4},{12,8},{16,12},{20,16},{24,20},{28,24},{5,1},{9,5},{13... | collective-permute-start | bytes 196616 | tf_op jit(solution)/shard_map/ppermute | solution.py:18
  18.3 3.8 %collective-permute-start.2 = (bf16[3,16,1,1024]{3,2,1,0:T(2,128)(2,1)S(1)}, bf16[3,16,1,1024]{3,2,1,0:T(2,128)(2,1)S(1)}, u32[]{:S(2)}, u32[]{:S(2)}) collective-permute-start(bf16[3,16,1,1024]{3,2,1,0:T(2,128)(2,1)S(1)} %get-tuple-element.19), channel_id=1, source_target_pairs={{0,1},{1,2},{2,3},{4,5},{5,6},{6,7},{8,9},{9,10},{10,11},{12,13},{... | collective-permute-start | bytes 294920 | tf_op jit(solution)/shard_map/ppermute | solution.py:17
  19.6 5.1 %collective-permute-start.3 = (bf16[3,16,1,1024]{3,2,1,0:T(2,128)(2,1)S(1)}, bf16[3,16,1,1024]{3,2,1,0:T(2,128)(2,1)S(1)}, u32[]{:S(2)}, u32[]{:S(2)}) collective-permute-start(bf16[3,16,1,1024]{3,2,1,0:T(2,128)(2,1)S(1)} %get-tuple-element.20), channel_id=1, source_target_pairs={{1,0},{2,1},{3,2},{5,4},{6,5},{7,6},{9,8},{10,9},{11,10},{13,12},{... | collective-permute-start | bytes 294920 | tf_op jit(solution)/shard_map/ppermute | solution.py:18
  38.0 65.7 %reduce-scatter.2.cloned.1.call-start = ((), (), s32[]{:S(2)}) async-start(), calls=%async_computation.2 | async-start | bytes 655360 | tf_op jit(solution)/shard_map/reduce_scatter | solution.py:96
  78.7 2.2 %copy-start.3 = (bf16[1024,8,64]{0,2,1:T(8,128)(2,1)S(1)}, bf16[1024,8,64]{0,2,1:T(8,128)(2,1)}, u32[]{:S(2)}) copy-start(bf16[1024,8,64]{0,2,1:T(8,128)(2,1)} %all-gather.2.cloned.1.call-done) | copy-start | bytes 3145732
  80.9 1.0 copy-start.1
Sparse Core Ops, SparseCore 0:
  38.1 40.5 all-gather.1
  83.1 20.5 reduce-scatter.1
